TPU v7x, 128 devices: a whole 4x4x4 slice. The times are simulated.
128 devices in a mesh: seq: 32 (over x, z, core), tp: 4 (over y).
Axes of the slice: x: 4, y: 4, z: 4, core: 2. Of those that a mesh axis runs over, the one named last changes fastest.
Arguments:
- tokens: bfloat16 [8192, 2048], P('seq'), may hold values from -6 to 6
- norm_gain: float32 [2048], replicated, may hold values from 0.1 to 1.9
- qkv_weight: bfloat16 [2048, 4096], P(None, 'tp'), may hold values from -0.125 to 0.125
- conv_weight: float32 [4, 4096], P(None, 'tp'), may hold values from -3 to 3
- gate_down: bfloat16 [2048, 16], replicated, may hold values from -0.125 to 0.125
- gate_up: bfloat16 [16, 1024], P(None, 'tp'), may hold values from -6 to 6
- gate_bias: float32 [1024], P('tp'), may hold values from 0.3 to 8.5
- out_gate_weight: bfloat16 [2048, 2048], P(None, 'tp'), may hold values from -0.125 to 0.125
- head_gain: float32 [512], replicated, may hold values from 0.1 to 1.9
- out_weight: bfloat16 [2048, 2048], P('tp'), may hold values from -0.125 to 0.125
- final_gain: float32 [2048], replicated, may hold values from 0.1 to 1.9
- embedding: bfloat16 [32000, 2048], P(('seq', 'tp')), may hold values from -0.5 to 0.5
- lengths: int32 [8], replicated, may hold values from 1 to 4096, as said below
- packed_order: int32 [8], replicated, may hold values from 0 to 7, each once
Outputs:
- hidden: bfloat16 [8192, 2048], P('seq', 'tp')
- last_states: float32 [8, 4, 256, 512], P(None, 'tp')
- conv_edges: float32 [8, 3, 4096], P(None, None, 'tp')
- last_norms: float32 [8], replicated
- max_logits: float32 [8, 128], P(None, ('seq', 'tp'))
Inputs may be any that keep to these rules, and one draw needn't show every extreme that they name: Request r of the initial order has lengths[r] tokens; the lengths sum to 8192, the largest is 4096 and the smallest is 1 or 2. packed_order names every request once; the packed positions hold the tokens of request packed_order[0], then those of packed_order[1], and so on.
All inputs are finite; a program needn't handle non-finite values.
Results may differ from a plain program's by a relative error of at most 0.015.
Values may be sent and summed in bfloat16 or wider, within the bound.
No kernel may reach another device: no remote copies, remote signals or barrier semaphores. Data moves between devices by JAX's collectives and lax.ppermute only.
A program may use at most 128 MiB of HBM per device.

v0:
```python
from functools import partial
import jax
import jax.numpy as jnp
from jax import lax
from jax.sharding import PartitionSpec as P

DK = 256
DV = 512
KCONV = 4
BLOCK = 64
HIGHEST_PRECISION = lax.Precision.HIGHEST


def prefix(array, axis, combine, identity):
    peers, place = (lax.axis_size(axis), lax.axis_index(axis))
    everything = jax.tree.map(
        lambda part, kind: lax.all_gather(part.astype(kind), axis),
        array,
        (jnp.bfloat16, jnp.bfloat16),
    )
    start = jax.tree.map(
        lambda part, zero: jnp.broadcast_to(jnp.asarray(zero, part.dtype), part.shape),
        array,
        identity,
    )

    def hop(k, before):
        reached = k < place
        new = combine(
            before, jax.tree.map(lambda part, own: part[k].astype(own.dtype), everything, array)
        )
        return jax.tree.map(lambda a, b: jnp.where(reached, a, b), new, before)

    return lax.fori_loop(0, peers, hop, start)


def passed_along(array, axis, by):
    peers = lax.axis_size(axis)
    pairs = [(i, i + by) for i in range(peers) if 0 <= i + by < peers]
    return lax.ppermute(array, axis, pairs)


def segments(lengths, packed_order, positions):
    request_count = lengths.shape[0]
    select = (packed_order[:, None] == jnp.arange(request_count, dtype=jnp.int32)[None, :]).astype(
        jnp.int32
    )
    packed_len = jnp.sum(select * lengths[None, :], axis=1)
    end_points = jnp.cumsum(packed_len)
    starts = end_points - packed_len
    segment = jnp.sum((positions[:, None] >= starts[None, :]).astype(jnp.int32), axis=1) - 1
    last_index = jnp.sum(select * (end_points - 1)[:, None], axis=0)
    return (segment, last_index)


def causal_conv(padded, padded_segment, conv_weight, row_count):
    running = jnp.zeros((row_count, padded.shape[1]), jnp.float32)
    current = padded_segment[KCONV - 1 :]
    for offset in range(KCONV):
        window = padded[offset : offset + row_count]
        same_segment = (padded_segment[offset : offset + row_count] == current)[:, None]
        running = running + jnp.where(same_segment, window, 0.0) * conv_weight[offset]
    return running


def activate(convolved, head_count):
    shaped = convolved.reshape(convolved.shape[0], head_count, 2 * DK + DV)
    channel = jnp.arange(2 * DK + DV)
    return jnp.where(channel < 2 * DK, jax.nn.silu(shaped), shaped).astype(jnp.bfloat16)


def advance(carry_state, key_floats, values, cumulative, segment, segment_before):
    total_decay = cumulative[-1]
    same_tail = (segment == segment[-1])[:, None, None]
    scaled = jnp.where(same_tail, key_floats * jnp.exp(total_decay[None] - cumulative), 0.0).astype(
        jnp.bfloat16
    )
    added = jnp.einsum("jhc,jhv->hcv", scaled, values, preferred_element_type=jnp.float32)
    through = segment[-1] == segment_before
    return jnp.where(through, jnp.exp(total_decay)[:, :, None] * carry_state, 0.0) + added


def state_at_ends(
    end_states, carry_state, key_floats, values, cumulative, segment, segment_before, offset
):
    length = segment.shape[0]
    inside_block = (offset >= 0) & (offset < length)

    def add_ends(previous):
        end_row = jnp.clip(offset, 0, length - 1)
        end_decay = cumulative[end_row]
        end_segment = segment[end_row]
        indices = jnp.arange(length)
        allowed = (
            (indices[None, :] <= end_row[:, None]) & (segment[None, :] == end_segment[:, None])
        )[:, :, None, None]
        spread = jnp.where(allowed, end_decay[:, None] - cumulative[None], 0.0)
        weighted = jnp.where(allowed, key_floats[None] * jnp.exp(spread), 0.0).astype(jnp.bfloat16)
        within = jnp.einsum("rjhc,jhv->rhcv", weighted, values, preferred_element_type=jnp.float32)
        carried = (end_segment == segment_before)[:, None, None, None]
        reached = jnp.where(carried, jnp.exp(end_decay)[:, :, :, None] * carry_state[None], 0.0)
        return jnp.where(inside_block[:, None, None, None], within + reached, previous)

    def keep(previous):
        return previous

    return lax.cond(jnp.any(inside_block), add_ends, keep, end_states)


def block_step(last_index, carry, inputs):
    carry_state, end_states = carry
    queries, key_rows, values, decays, segment, segment_before, block_first = inputs
    cumulative = jnp.cumsum(decays, axis=0)
    length = segment.shape[0]
    indices = jnp.arange(length)
    causal = (indices[None, :] <= indices[:, None]) & (segment[None, :] == segment[:, None])
    allowed = causal[:, :, None, None]
    spread = jnp.where(allowed, cumulative[:, None] - cumulative[None, :], 0.0)
    weights = jnp.where(allowed, jnp.exp(spread), 0.0)
    query_rows = queries.astype(jnp.float32)
    key_floats = key_rows.astype(jnp.float32)
    scores = jnp.sum(query_rows[:, None] * key_floats[None, :] * weights, axis=-1).astype(
        jnp.bfloat16
    )
    inside = jnp.einsum("ijh,jhv->ihv", scores, values, preferred_element_type=jnp.float32)
    carried = (segment == segment_before)[:, None, None]
    outside = jnp.einsum(
        "ihc,hcv->ihv", query_rows * jnp.exp(cumulative), carry_state, precision=HIGHEST_PRECISION
    )
    output = inside + jnp.where(carried, outside, 0.0)
    new_state = advance(carry_state, key_floats, values, cumulative, segment, segment_before)
    end_states = state_at_ends(
        end_states,
        carry_state,
        key_floats,
        values,
        cumulative,
        segment,
        segment_before,
        last_index - block_first,
    )
    return ((new_state, end_states), output)


def state_only(carry_state, inputs):
    block_queries, block_keys, block_values, block_decays, block_segment, before, block_start = (
        inputs
    )
    cumulative = jnp.cumsum(block_decays, axis=0)
    return (
        advance(
            carry_state,
            block_keys.astype(jnp.float32),
            block_values,
            cumulative,
            block_segment,
            before,
        ),
        None,
    )


def head_output(attended, gate_out, head_gain):
    row_count, head_count, value_width = attended.shape
    mean_square = jnp.mean(attended * attended, axis=2, keepdims=True)
    gate_values = jax.nn.silu(
        gate_out.astype(jnp.float32).reshape(row_count, head_count, value_width)
    )
    gated = attended * lax.rsqrt(mean_square + 1e-05) * head_gain * gate_values
    return gated.reshape(row_count, head_count * value_width).astype(jnp.bfloat16)


def carry_in(decay_factor, local_state):

    def combine(earlier, later):
        return (earlier[0] * later[0], later[0][:, :, None] * earlier[1] + later[1])

    identity = (jnp.ones_like(decay_factor), jnp.zeros_like(local_state))
    result = prefix((decay_factor, local_state), "seq", combine, identity)
    return result[1]


def shards(
    tokens,
    norm_gain,
    qkv_weight,
    conv_weight,
    gate_down,
    gate_up,
    gate_bias,
    out_gate_weight,
    head_gain,
    out_weight,
    final_gain,
    embedding,
    lengths,
    packed_order,
):
    row_count = tokens.shape[0]
    head_count = out_weight.shape[0] // DV
    column_count = tokens.shape[1] // lax.axis_size("tp")
    start_row = lax.axis_index("seq") * row_count
    positions = start_row + jnp.arange(-(KCONV - 1), row_count, dtype=jnp.int32)
    segment_all, last_index = segments(lengths, packed_order, positions)
    segment = segment_all[KCONV - 1 :]
    segment_prior = segment_all[KCONV - 2]
    first_index = last_index - lengths + 1
    residual = tokens.astype(jnp.float32)
    normed = (
        residual
        * lax.rsqrt(jnp.mean(residual * residual, axis=1, keepdims=True) + 1e-06)
        * norm_gain
    ).astype(jnp.bfloat16)
    projected = jnp.dot(normed, qkv_weight, preferred_element_type=jnp.float32).astype(jnp.bfloat16)
    rim_rows = passed_along(projected[row_count - (KCONV - 1) :], "seq", 1)
    padded = jnp.concatenate([rim_rows, projected], axis=0)
    convolved = causal_conv(padded.astype(jnp.float32), segment_all, conv_weight, row_count)
    activated = activate(convolved, head_count)
    queries = activated[:, :, :DK]
    key_rows = activated[:, :, DK : 2 * DK]
    values = activated[:, :, 2 * DK :]
    lowrank = jnp.dot(normed, gate_down, preferred_element_type=jnp.float32)
    gate_logits = (
        jnp.dot(lowrank, gate_up.astype(jnp.float32), precision=HIGHEST_PRECISION) + gate_bias
    )
    decays = (jax.nn.log_sigmoid(gate_logits) / 16.0).reshape(row_count, head_count, DK)
    gate_out = jnp.dot(normed, out_gate_weight, preferred_element_type=jnp.float32).astype(
        jnp.bfloat16
    )
    block_count = row_count // BLOCK

    def split_blocks(array):
        return array.reshape((block_count, BLOCK) + array.shape[1:])

    segment_before = segment_all[KCONV - 2 : KCONV - 2 + row_count : BLOCK]
    block_first = start_row + jnp.arange(block_count, dtype=jnp.int32) * BLOCK
    block_inputs = (
        split_blocks(queries),
        split_blocks(key_rows),
        split_blocks(values),
        split_blocks(decays),
        split_blocks(segment),
        segment_before,
        block_first,
    )
    through_shard = segment[-1] == segment_prior
    empty_state = jnp.zeros((head_count, DK, DV), jnp.float32)
    empty_ends = jnp.zeros((lengths.shape[0], head_count, DK, DV), jnp.float32)
    stepper = partial(block_step, last_index)
    local_state, unused_steps = lax.scan(state_only, empty_state, block_inputs)
    decay_factor = jnp.where(through_shard, jnp.exp(jnp.sum(decays, axis=0)), 0.0)
    incoming = carry_in(decay_factor, local_state)
    (unused_state, end_states), attended = lax.scan(stepper, (incoming, empty_ends), block_inputs)
    attended = attended.reshape(row_count, head_count, DV)
    gated = head_output(attended, gate_out, head_gain)
    projected_out = jnp.dot(gated, out_weight, preferred_element_type=jnp.float32)
    summed = lax.psum_scatter(
        projected_out.astype(jnp.bfloat16), "tp", scatter_dimension=1, tiled=True
    ).astype(jnp.float32)
    column_start = lax.axis_index("tp") * column_count
    own_columns = lax.dynamic_slice_in_dim(residual, column_start, column_count, 1)
    hidden = (own_columns + summed).astype(jnp.bfloat16)
    owned_here = (last_index >= start_row) & (last_index < start_row + row_count)
    local_last = jnp.clip(last_index - start_row, 0, row_count - 1)
    last_rows = jnp.where(owned_here[:, None], hidden[local_last].astype(jnp.float32), 0.0)
    edge_list = []
    for offset in range(KCONV - 1):
        located = last_index - (KCONV - 2) + offset
        inside = owned_here & (located >= first_index)
        picked = padded[jnp.clip(located - start_row + KCONV - 1, 0, row_count + KCONV - 2)].astype(
            jnp.float32
        )
        edge_list.append(jnp.where(inside[:, None], picked, 0.0))
    conv_edges = jnp.stack(edge_list, axis=1)
    row_sums, conv_edges, last_states = (
        lax.psum(last_rows.astype(jnp.bfloat16), "seq").astype(jnp.float32),
        lax.psum(conv_edges.astype(jnp.bfloat16), "seq").astype(jnp.float32),
        lax.psum(end_states.astype(jnp.bfloat16), "seq").astype(jnp.float32),
    )
    full_rows = lax.all_gather(row_sums, "tp", axis=1, tiled=True)
    mean_square = jnp.mean(full_rows * full_rows, axis=1)
    last_norms = jnp.sqrt(mean_square)
    final_rows = (full_rows * lax.rsqrt(mean_square[:, None] + 1e-06) * final_gain).astype(
        jnp.bfloat16
    )
    logits = jnp.dot(final_rows, embedding.T, preferred_element_type=jnp.float32)
    max_logits = jnp.max(logits, axis=1, keepdims=True)
    return (hidden, last_states, conv_edges, last_norms, max_logits)


def solution(mesh):
    in_specs = (
        P("seq", None),
        P(),
        P(None, "tp"),
        P(None, "tp"),
        P(),
        P(None, "tp"),
        P("tp"),
        P(None, "tp"),
        P(),
        P("tp", None),
        P(),
        P(("seq", "tp"), None),
        P(),
        P(),
    )
    out_specs = (
        P("seq", "tp"),
        P(None, "tp", None, None),
        P(None, None, "tp"),
        P(),
        P(None, ("seq", "tp")),
    )
    return jax.shard_map(shards, mesh=mesh, in_specs=in_specs, out_specs=out_specs, check_vma=False)
```

profile of v0, /device:TPU:0, one launch (start us, length us, event | category | flops | bytes accessed | tf_op | source)
XLA Modules:
  0.0 477.1 jit_solution(16728195551736005816)
XLA Ops:
  7.2 1.6 multiply_reduce_fusion.1
  9.0 3.9 convolution_convert_fusion.1
  12.9 1.3 collective-permute-start
  14.8 1.7 fusion.70
  17.2 1.0 copy.52
  18.2 1.0 pad_maximum_fusion
  21.1 21.8 %while.43 = (s32[]{:T(128)}, f32[1,256,512]{2,1,0:T(8,128)S(1)}, s32[4,64]{1,0:T(4,128)S(1)}, s32[4]{0:T(128)S(1)}, f32[4,64,1,256]{3,2,1,0:T(1,128)}, /*index=5...) while((s32[]{:T(128)}, f32[1,256,512]{2,1,0:T(8,128)S(1)}, ...), condition=%wide.region_7.8_spmd.clone, body=%wide.region_5.7_spmd.clone.sunk | while | flops 18415684 | bytes 1417237 | solution.py:250
  25.3 1.2 fusion.123
  30.8 1.2 fusion.123
  36.2 1.2 fusion.123
  41.7 1.2 fusion.123
  45.5 26.3 %all-gather.2 = bf16[32,1,256]{2,1,0:T(2,128)(2,1)S(1)} all-gather(bf16[1,1,256]{2,1,0:T(2,128)(2,1)S(1)} %reshape.975), channel_id=2, replica_groups=mesh['seq'=32,'tp'=4] {'seq'}, dimensions={0}, use_global_device_ids=true | all-gather | bytes 16896 | tf_op jit(solution)/shard_map/all_gather | solution.py:17
  71.9 29.0 %all-gather.5.cloned.1.call-done = bf16[32,256,512]{2,1,0:T(8,128)(2,1)} async-done(((bf16[1,256,512]{2,1,0:T(8,128)(2,1)}), bf16[32,256,512]{2,1,0:T(8,128)(2,1)}) %all-gather.5.cloned.1.call-update) | async-done | bytes 8388624 | tf_op jit(solution)/shard_map/all_gather | solution.py:17
  101.0 36.2 %while.44 = (s32[]{:T(128)}, f32[1,256,512]{2,1,0:T(8,128)S(1)}, s32[]{:T(128)}, bf16[32,1,256]{2,1,0:T(2,128)(2,1)S(1)}, bf16[32,1,256,512]{3,2,1,0:T(8,128)(2,1)}, /*index=5*/s32[]{:T(128)}, s32[]{:T(128)}) while((s32[]{:T(128)}, f32[1,256,512]{2,1,0:T(8,128)S(1)}, s32[]{:T(128)}, bf16[32,1,256]{2,1,0:T(2,128)(2,1)S(1)}, ...), condition=%wide.region_9.10_spmd.clone, body=%wide.region_8.9_spmd.clone.sunk | while | flops 655620 | bytes 1313385 | solution.py:34
  101.0 1.1 fusion.124
  102.1 1.1 fusion.124
  103.2 1.1 fusion.124
  104.4 1.1 fusion.124
  105.5 1.1 fusion.124
  106.6 1.1 fusion.124
  107.7 1.1 fusion.124
  108.9 1.1 fusion.124
  110.0 1.1 fusion.124
  111.1 1.1 fusion.124
  112.3 1.1 fusion.124
  113.4 1.1 fusion.124
  114.5 1.1 fusion.124
  115.7 1.1 fusion.124
  116.8 1.1 fusion.124
  117.9 1.1 fusion.124
  119.1 1.1 fusion.124
  120.2 1.1 fusion.124
  121.3 1.1 fusion.124
  122.5 1.1 fusion.124
  123.6 1.1 fusion.124
  124.7 1.1 fusion.124
  125.9 1.1 fusion.124
  127.0 1.1 fusion.124
  128.1 1.1 fusion.124
  129.2 1.1 fusion.124
  130.4 1.1 fusion.124
  131.5 1.1 fusion.124
  132.6 1.1 fusion.124
  133.8 1.1 fusion.124
  134.9 1.1 fusion.124
  136.0 1.1 fusion.124
  137.1 1.5 broadcast_in_dim.240
  138.6 54.6 %while.42 = (s32[]{:T(128)}, f32[1,256,512]{2,1,0:T(8,128)S(1)}, bf16[8,1,256,512]{3,2,0,1:T(8,128)(2,1)}, f32[4,64,1,512]{3,1,2,0:T(8,128)}, s32[4,64]{1,0:T(4,...) while((s32[]{:T(128)}, f32[1,256,512]{2,1,0:T(8,128)S(1)}, ...), condition=%wide.region_17.18_spmd, body=%wide.region_11.17_spmd.sunk | while | flops 268659424 | bytes 8804605 | solution.py:253
  144.4 5.7 %conditional.2 = (bf16[8,1,256,512]{3,2,0,1:T(8,128)(2,1)}) conditional(s32[]{:T(128)} %convert_element_type.388, bf16[8,1,256,512]{3,2,0,1:T(8,128)(2,1)} %get-tuple-element.722, (pred[8]{0:T(512)(128)(4,1)S(1)}, s32[8]{0:T(128)S(1)}, s32[64]{0:T(128)S(1)}, bf16[1,64,1,256]{3,2,1,0:T(2,128)(2,1)S(1)}, f32[64,1,256]{2,1,0:T(1,128)S(1)}, ...), branch_computations={%region_14.14_spmd, %region_15.15_spmd} | conditional | flops 139086368 | bytes 5199492 | solution.py:107
  146.4 3.7 fusion
  150.3 2.0 multiply_reduce_fusion.5
  162.5 2.0 multiply_reduce_fusion.5
  174.7 2.0 multiply_reduce_fusion.5
  187.0 2.0 multiply_reduce_fusion.5
  194.5 2.8 fusion.56
  197.3 1.7 convolution_convert_fusion
  199.0 2.8 convert_element_type.287
  203.9 96.7 %all-reduce.3.cloned.1.call-done = bf16[8,1,256,512]{3,2,1,0:T(8,128)(2,1)} async-done(((bf16[8,1,256,512]{3,2,1,0:T(8,128)(2,1)}), bf16[8,1,256,512]{3,2,1,0:T(8,128)(2,1)}) %all-reduce.3.cloned.1.call-update) | async-done | bytes 2097168 | tf_op jit(solution)/shard_map/psum | solution.py:278
  300.6 4.2 convert_element_type.304
  304.8 21.7 %reduce-scatter.2.cloned.1.call-done = bf16[256,512]{1,0:T(8,128)(2,1)} async-done(((bf16[256,2048]{1,0:T(8,128)(2,1)}), bf16[256,512]{1,0:T(8,128)(2,1)}) %reduce-scatter.2.cloned.1.call-update) | async-done | bytes 262160 | tf_op jit(solution)/shard_map/reduce_scatter | solution.py:257
  326.5 1.2 add_convert_fusion
  328.3 126.8 %all-reduce = (bf16[8,3,1024]{2,0,1:T(8,128)(2,1)S(1)}, bf16[8,512]{1,0:T(8,128)(2,1)S(1)}) all-reduce(bf16[8,3,1024]{2,0,1:T(8,128)(2,1)S(1)} %pad_maximum_fusion.1, bf16[8,512]{1,0:T(8,128)(2,1)S(1)} %select_convert_fusion.2), channel_id=1, replica_groups=mesh['seq'=32,'tp'=4] {'seq'}, use_global_device_ids=true, to_apply=%region_21.22 | all-reduce | flops 28672 | bytes 114688 | tf_op jit(solution)/shard_map/psum | solution.py:277
  455.2 11.9 %all_gather.16 = f32[8,2048]{1,0:T(8,128)S(1)} all-gather(f32[8,512]{1,0:T(8,128)S(1)} %convert_element_type.314), channel_id=1, replica_groups=mesh['seq'=32,'tp'=4] {'tp'}, dimensions={1}, use_global_device_ids=true | all-gather | bytes 81920 | tf_op jit(solution)/shard_map/all_gather | solution.py:280
  468.3 2.2 convolution_reduce_fusion
  (243 shorter events, 56.2 us)
Async XLA Ops:
  7.2 190.1 %copy-start = (bf16[512,2048]{1,0:T(8,128)(2,1)S(1)}, bf16[512,2048]{1,0:T(8,128)(2,1)}, u32[]{:S(2)}) copy-start(bf16[512,2048]{1,0:T(8,128)(2,1)} %param.31) | copy-start | bytes 6291460
  7.2 93.8 %all-gather.5.cloned.1.call-start = ((), (), s32[]{:S(2)}) async-start(), calls=%async_computation.3 | async-start | bytes 8650752 | tf_op jit(solution)/shard_map/all_gather | solution.py:17
  8.9 5.3 %copy-start.6 = (s32[8]{0:T(128)S(1)}, s32[8]{0:T(128)}, u32[]{:S(2)}) copy-start(s32[8]{0:T(128)} %param.34) | copy-start | bytes 100
  8.9 5.3 %copy-start.12 = (s32[8]{0:T(128)S(1)}, s32[8]{0:T(128)}, u32[]{:S(2)}) copy-start(s32[8]{0:T(128)} %param.35) | copy-start | bytes 100
  8.9 5.8 %copy-start.4 = (f32[4,1024]{1,0:T(4,128)S(1)}, f32[4,1024]{1,0:T(4,128)}, u32[]{:S(2)}) copy-start(f32[4,1024]{1,0:T(4,128)} %param.25) | copy-start | bytes 49156
  8.9 5.8 %copy-start.7 = (bf16[2048,16]{0,1:T(8,128)(2,1)S(1)}, bf16[2048,16]{0,1:T(8,128)(2,1)}, u32[]{:S(2)}) copy-start(bf16[2048,16]{0,1:T(8,128)(2,1)} %param.26) | copy-start | bytes 196612
  8.9 5.8 %copy-start.9 = (f32[2048]{0:T(1024)S(1)}, f32[2048]{0:T(1024)}, u32[]{:S(2)}) copy-start(f32[2048]{0:T(1024)} %param.23) | copy-start | bytes 24580
  8.9 7.5 %copy-start.8 = (bf16[16,256]{1,0:T(8,128)(2,1)S(1)}, bf16[16,256]{1,0:T(8,128)(2,1)}, u32[]{:S(2)}) copy-start(bf16[16,256]{1,0:T(8,128)(2,1)} %param.27) | copy-start | bytes 24580
  9.0 7.5 %copy-start.11 = (f32[256]{0:T(256)S(1)}, f32[256]{0:T(256)}, u32[]{:S(2)}) copy-start(f32[256]{0:T(256)} %param.28) | copy-start | bytes 3076
  12.9 5.3 %collective-permute-start = (bf16[3,1024]{1,0:T(4,128)(2,1)S(1)}, bf16[3,1024]{1,0:T(4,128)(2,1)S(1)}, u32[]{:S(2)}, u32[]{:S(2)}) collective-permute-start(bf16[3,1024]{1,0:T(4,128)(2,1)S(1)} %slice.111), channel_id=1, source_target_pairs={{0,4},{4,8},{8,12},{12,16},{16,20},{20,24},{24,28},{28,32},{32,36}... | collective-permute-start | bytes 18440 | tf_op jit(solution)/shard_map/ppermute | solution.py:40
  43.6 257.0 %all-reduce.3.cloned.1.call-start = ((), (), s32[]{:S(2)}) async-start(), calls=%async_computation.2 | async-start | bytes 4194304 | tf_op jit(solution)/shard_map/psum | solution.py:278
  193.3 1.0 copy-start.2
  193.3 1.2 copy-start.10
  193.3 133.2 %reduce-scatter.2.cloned.1.call-start = ((), (), s32[]{:S(2)}) async-start(), calls=%async_computation.1 | async-start | bytes 1310720 | tf_op jit(solution)/shard_map/reduce_scatter | solution.py:257
  199.0 2.9 copy-start.1
  203.9 264.4 %copy-start.5 = (f32[2048]{0:T(1024)S(1)}, f32[2048]{0:T(1024)}, u32[]{:S(2)}) copy-start(f32[2048]{0:T(1024)} %param.32) | copy-start | bytes 24580
  327.7 142.9 %copy-start.3 = (bf16[256,512]{1,0:T(8,128)(2,1)}, bf16[256,512]{1,0:T(8,128)(2,1)S(1)}, u32[]{:S(2)}) copy-start(bf16[256,512]{1,0:T(8,128)(2,1)S(1)} %add_convert_fusion) | copy-start | bytes 786436
Sparse Core Ops, SparseCore 0:
  43.7 57.1 all-gather.4
  193.4 107.1 all-reduce.2
  303.0 23.4 reduce-scatter.1
where the time goes:
time: 480 us; the launch traced here: 477 us
  blocking collectives  165 us (34%)
  waiting for transfers between devices  147 us (31%)
  other arithmetic  81.7 us (17%)
  matrix products  27.2 us (6%)
  local copies, waits for them, and re-layouts  24.3 us (5%)
  between operations  15.3 us (3%)
  loops' own time  14.8 us (3%)
    psum x1, blocking collectives, shards(): lax.psum(conv_edges.astype(jnp.bfloat16), 'seq').astype(jnp.float32)  127 us
    psum x1, waiting for transfers between devices, shards(): lax.psum(end_states.astype(jnp.bfloat16), 'seq').astype(jnp.float32)  96.7 us
    select_n x32, other arithmetic, hop(): return jax.tree.map(lambda a, b: jnp.where(reached, a, b), new, before)  34.9 us
    all_gather x1, waiting for transfers between devices, prefix(): lax.all_gather(part.astype(kind), axis)  29 us
    all_gather x1, blocking collectives, prefix(): lax.all_gather(part.astype(kind), axis)  26.3 us
    reduce_scatter x1, waiting for transfers between devices, shards(): lax.psum_scatter(projected_out.astype(jnp.bfloat16), 'tp', scatter_dimens...  21.7 us
    all_gather x1, blocking collectives, shards(): full_rows = lax.all_gather(row_sums, 'tp', axis=1, tiled=True)  11.9 us
    dynamic_slice x24, local copies, waits for them, and re-layouts, shards(): local_state, unused_steps = lax.scan(state_only, empty_state, block_inputs)  10.5 us
  transfers between devices with their start and end apart: 4, of which 3 were waited for; matrix products, arithmetic and copies ran while one was open for 4% of the time, Pallas kernels for 0%

commit v1 on v0

--- a/solution.py
+++ b/solution.py
@@ -277,7 +277,9 @@
         lax.psum(conv_edges.astype(jnp.bfloat16), "seq").astype(jnp.float32),
         lax.psum(end_states.astype(jnp.bfloat16), "seq").astype(jnp.float32),
     )
-    full_rows = lax.all_gather(row_sums, "tp", axis=1, tiled=True)
+    full_rows = jnp.concatenate(
+        lax.all_to_all(jnp.stack([row_sums] * lax.axis_size("tp")), "tp", 0, 0), axis=1
+    )
     mean_square = jnp.mean(full_rows * full_rows, axis=1)
     last_norms = jnp.sqrt(mean_square)
     final_rows = (full_rows * lax.rsqrt(mean_square[:, None] + 1e-06) * final_gain).astype(

time: 480 us -> 372 us (0.78)
  waiting for transfers between devices: 147 us -> 45.3 us
  blocking collectives: 165 us -> 154 us
    psum x1, waiting for transfers between devices: 96.7 us -> 0.02 us  [shards(): lax.psum(end_states.astype(jnp.bfloat16), 'seq').astype(jnp.float32)]
    all_gather x1 -> x0, blocking collectives: 11.9 us -> none  [shards(): full_rows = lax.all_gather(row_sums, 'tp', axis=1, tiled=True)]
    reduce_scatter x1, waiting for transfers between devices: 21.7 us -> 16.3 us  [shards(): lax.psum_scatter(projected_out.astype(jnp.bfloat16), 'tp', scatter_dimens...]
  transfers between devices with their start and end apart: 4 -> 5, of which waited for: 3 -> 3; matrix products, arithmetic and copies ran while one was open for 4% -> 5% of each run, Pallas kernels for 0% -> 0%
where the time goes in v1:
time: 372 us; the launch traced here: 370 us
  blocking collectives  154 us (41%)
  other arithmetic  82.6 us (22%)
  waiting for transfers between devices  45.3 us (12%)
  local copies, waits for them, and re-layouts  28.1 us (8%)
  matrix products  24.8 us (7%)
  between operations  15.3 us (4%)
  loops' own time  14.8 us (4%)
  starting transfers between devices  4.69 us (1%)
    psum x1, blocking collectives, shards(): lax.psum(conv_edges.astype(jnp.bfloat16), 'seq').astype(jnp.float32)  127 us
    select_n x32, other arithmetic, hop(): return jax.tree.map(lambda a, b: jnp.where(reached, a, b), new, before)  34.9 us
    all_gather x1, waiting for transfers between devices, prefix(): lax.all_gather(part.astype(kind), axis)  28.3 us
    all_gather x1, blocking collectives, prefix(): lax.all_gather(part.astype(kind), axis)  27 us
    reduce_scatter x1, waiting for transfers between devices, shards(): lax.psum_scatter(projected_out.astype(jnp.bfloat16), 'tp', scatter_dimens...  16.3 us
    dynamic_slice x24, local copies, waits for them, and re-layouts, shards(): local_state, unused_steps = lax.scan(state_only, empty_state, block_inputs)  10.5 us
    another operation x1, loops' own time, shards(): lax.scan(stepper, (incoming, empty_ends), block_inputs)  8.29 us
    reduce_sum x4, other arithmetic, block_step(): jnp.sum(query_rows[:, None] * key_floats[None, :] * weights, axis=-1)  8.17 us
  transfers between devices with their start and end apart: 5, of which 3 were waited for; matrix products, arithmetic and copies ran while one was open for 5% of the time, Pallas kernels for 0%

profile of v1, /device:TPU:0, one launch (start us, length us, event | category | flops | bytes accessed | tf_op | source)
XLA Modules:
  0.0 369.8 jit_solution(17331438721502687646)
XLA Ops:
  7.2 1.6 multiply_reduce_fusion.1
  9.0 3.9 %convolution_convert_fusion.1 = bf16[256,1024]{1,0:T(8,128)(2,1)S(1)} fusion(bf16[2048,1024]{1,0:T(8,128)(2,1)} %param.24, f32[2048]{0:T(1024)} %param.23, f32[256]{0:T(256)S(1)} %add_rsqrt_fusion.1, bf16[256,2048]{1,0:T(8,128)(2,1)} %param.22), kind=kOutput, calls=%fused_computation.94 | convolution fusion | flops 1076101120 | bytes 5776384 | tf_op jit(solution)/shard_map/dot_general | solution.py:214
  13.7 1.3 collective-permute-start
  17.8 2.1 pad_maximum_fusion
  21.7 21.8 %while.43 = (s32[]{:T(128)}, f32[1,256,512]{2,1,0:T(8,128)S(1)}, s32[4,64]{1,0:T(4,128)S(1)}, s32[4]{0:T(128)S(1)}, f32[4,64,1,256]{3,2,1,0:T(1,128)}, /*index=5...) while((s32[]{:T(128)}, f32[1,256,512]{2,1,0:T(8,128)S(1)}, ...), condition=%wide.region_7.8_spmd.clone, body=%wide.region_5.7_spmd.clone.sunk | while | flops 18415684 | bytes 1417237 | solution.py:250
  26.0 1.2 fusion.124
  31.4 1.2 fusion.124
  36.9 1.2 fusion.124
  42.3 1.2 fusion.124
  46.2 27.0 %all-gather.2 = bf16[32,1,256]{2,1,0:T(2,128)(2,1)S(1)} all-gather(bf16[1,1,256]{2,1,0:T(2,128)(2,1)S(1)} %reshape.985), channel_id=2, replica_groups=mesh['seq'=32,'tp'=4] {'seq'}, dimensions={0}, use_global_device_ids=true | all-gather | bytes 16896 | tf_op jit(solution)/shard_map/all_gather | solution.py:17
  73.3 28.3 %all-gather.5.cloned.1.call-done = bf16[32,256,512]{2,1,0:T(8,128)(2,1)} async-done(((bf16[1,256,512]{2,1,0:T(8,128)(2,1)}), bf16[32,256,512]{2,1,0:T(8,128)(2,1)}) %all-gather.5.cloned.1.call-update) | async-done | bytes 8388624 | tf_op jit(solution)/shard_map/all_gather | solution.py:17
  101.6 36.2 %while.44 = (s32[]{:T(128)}, f32[1,256,512]{2,1,0:T(8,128)S(1)}, s32[]{:T(128)}, bf16[32,1,256]{2,1,0:T(2,128)(2,1)S(1)}, bf16[32,1,256,512]{3,2,1,0:T(8,128)(2,1)}, /*index=5*/s32[]{:T(128)}, s32[]{:T(128)}) while((s32[]{:T(128)}, f32[1,256,512]{2,1,0:T(8,128)S(1)}, s32[]{:T(128)}, bf16[32,1,256]{2,1,0:T(2,128)(2,1)S(1)}, ...), condition=%wide.region_9.10_spmd.clone, body=%wide.region_8.9_spmd.clone.sunk | while | flops 655620 | bytes 1313385 | solution.py:34
  101.6 1.1 fusion.125
  102.7 1.1 fusion.125
  103.9 1.1 fusion.125
  105.0 1.1 fusion.125
  106.1 1.1 fusion.125
  107.3 1.1 fusion.125
  108.4 1.1 fusion.125
  109.5 1.1 fusion.125
  110.7 1.1 fusion.125
  111.8 1.1 fusion.125
  112.9 1.1 fusion.125
  114.0 1.1 fusion.125
  115.2 1.1 fusion.125
  116.3 1.1 fusion.125
  117.4 1.1 fusion.125
  118.6 1.1 fusion.125
  119.7 1.1 fusion.125
  120.8 1.1 fusion.125
  122.0 1.1 fusion.125
  123.1 1.1 fusion.125
  124.2 1.1 fusion.125
  125.4 1.1 fusion.125
  126.5 1.1 fusion.125
  127.6 1.1 fusion.125
  128.8 1.1 fusion.125
  129.9 1.1 fusion.125
  131.0 1.1 fusion.125
  132.2 1.1 fusion.125
  133.3 1.1 fusion.125
  134.4 1.1 fusion.125
  135.5 1.1 fusion.125
  136.7 1.1 fusion.125
  137.8 1.5 broadcast_in_dim.240
  139.3 54.6 %while.42 = (s32[]{:T(128)}, f32[1,256,512]{2,1,0:T(8,128)S(1)}, bf16[8,1,256,512]{3,2,0,1:T(8,128)(2,1)}, f32[4,64,1,512]{3,1,2,0:T(8,128)}, s32[4,64]{1,0:T(4,...) while((s32[]{:T(128)}, f32[1,256,512]{2,1,0:T(8,128)S(1)}, ...), condition=%wide.region_17.18_spmd, body=%wide.region_11.17_spmd.sunk | while | flops 268659424 | bytes 8804605 | solution.py:253
  145.0 5.8 %conditional.2 = (bf16[8,1,256,512]{3,2,0,1:T(8,128)(2,1)}) conditional(s32[]{:T(128)} %convert_element_type.388, bf16[8,1,256,512]{3,2,0,1:T(8,128)(2,1)} %get-tuple-element.722, (pred[8]{0:T(512)(128)(4,1)S(1)}, s32[8]{0:T(128)S(1)}, s32[64]{0:T(128)S(1)}, bf16[1,64,1,256]{3,2,1,0:T(2,128)(2,1)S(1)}, f32[64,1,256]{2,1,0:T(1,128)S(1)}, ...), branch_computations={%region_14.14_spmd, %region_15.15_spmd} | conditional | flops 139086368 | bytes 5199492 | solution.py:107
  147.1 3.7 %fusion = bf16[8,1,256,512]{3,2,0,1:T(8,128)(2,1)} fusion(bf16[8,1,256,512]{3,2,0,1:T(8,128)(2,1)} %get-tuple-element.210, f32[256,512]{1,0:T(8,128)S(1)} %bitcast.271, f32[8,256]{1,0:T(8,128)S(1)} %exp.116, pred[8]{0:T(512)(128)(4,1)S(1)} %broadcast_compare_fusion, pred[8]{0:T(512)(128)(4,1)S(1)} %get-tuple-element.202, f32[8,256]{1,0:T(8,128)S(1)} %gather_fusion.1, ...), kind=kOutput, calls=%fused_computation.7 | convolution fusion | flops 139067392 | bytes 4932112 | tf_op jit(solution)/shard_map/while/body/eval_jaxpr/cond/branch_1_fun/rjhc,jhv->rhcv/dot_general | solution.py:99
  150.9 2.0 multiply_reduce_fusion.4
  163.2 2.0 multiply_reduce_fusion.4
  175.4 2.0 multiply_reduce_fusion.4
  187.6 2.0 multiply_reduce_fusion.4
  193.9 1.2 multiply_reduce_fusion.2
  195.2 2.8 fusion.56
  198.0 1.7 convolution_convert_fusion
  199.8 1.5 convert_element_type.287
  201.5 1.7 gather_fusion.4
  203.2 1.7 gather_fusion.3
  204.9 1.7 gather_fusion.2
  206.8 16.3 %reduce-scatter.2.cloned.1.call-done = bf16[256,512]{1,0:T(8,128)(2,1)} async-done(((bf16[256,2048]{1,0:T(8,128)(2,1)}), bf16[256,512]{1,0:T(8,128)(2,1)}) %reduce-scatter.2.cloned.1.call-update) | async-done | bytes 262160 | tf_op jit(solution)/shard_map/reduce_scatter | solution.py:257
  223.1 1.2 add_convert_fusion
  225.0 127.1 %all-reduce = (bf16[8,3,1024]{2,0,1:T(8,128)(2,1)S(1)}, bf16[8,512]{1,0:T(8,128)(2,1)S(1)}) all-reduce(bf16[8,3,1024]{2,0,1:T(8,128)(2,1)S(1)} %pad_maximum_fusion.1, bf16[8,512]{1,0:T(8,128)(2,1)S(1)} %select_convert_fusion.2), channel_id=1, replica_groups=mesh['seq'=32,'tp'=4] {'seq'}, use_global_device_ids=true, to_apply=%region_21.22 | all-reduce | flops 28672 | bytes 114688 | tf_op jit(solution)/shard_map/psum | solution.py:277
  352.7 3.3 all-to-all-start
  356.1 4.3 %convert_element_type.304 = f32[8,1,256,512]{3,2,1,0:T(8,128)} convert(bf16[8,1,256,512]{3,2,1,0:T(8,128)(2,1)} %all-reduce.3.cloned.1.call-done) | non-fusion elementwise | flops 1048576 | bytes 6291456 | tf_op jit(solution)/shard_map/convert_element_type | solution.py:278
  (248 shorter events, 57.9 us)
Async XLA Ops:
  7.2 190.9 %copy-start = (bf16[512,2048]{1,0:T(8,128)(2,1)S(1)}, bf16[512,2048]{1,0:T(8,128)(2,1)}, u32[]{:S(2)}) copy-start(bf16[512,2048]{1,0:T(8,128)(2,1)} %param.31) | copy-start | bytes 6291460
  7.2 94.4 %all-gather.5.cloned.1.call-start = ((), (), s32[]{:S(2)}) async-start(), calls=%async_computation.4 | async-start | bytes 8650752 | tf_op jit(solution)/shard_map/all_gather | solution.py:17
  8.9 6.1 %copy-start.8 = (s32[8]{0:T(128)S(1)}, s32[8]{0:T(128)}, u32[]{:S(2)}) copy-start(s32[8]{0:T(128)} %param.34) | copy-start | bytes 100
  8.9 6.1 %copy-start.14 = (s32[8]{0:T(128)S(1)}, s32[8]{0:T(128)}, u32[]{:S(2)}) copy-start(s32[8]{0:T(128)} %param.35) | copy-start | bytes 100
  8.9 6.7 %copy-start.6 = (f32[4,1024]{1,0:T(4,128)S(1)}, f32[4,1024]{1,0:T(4,128)}, u32[]{:S(2)}) copy-start(f32[4,1024]{1,0:T(4,128)} %param.25) | copy-start | bytes 49156
  8.9 6.7 %copy-start.1 = (bf16[256,2048]{1,0:T(8,128)(2,1)S(1)}, bf16[256,2048]{1,0:T(8,128)(2,1)}, u32[]{:S(2)}) copy-start(bf16[256,2048]{1,0:T(8,128)(2,1)} %param.22) | copy-start | bytes 3145732
  8.9 6.7 %copy-start.9 = (bf16[2048,16]{0,1:T(8,128)(2,1)S(1)}, bf16[2048,16]{0,1:T(8,128)(2,1)}, u32[]{:S(2)}) copy-start(bf16[2048,16]{0,1:T(8,128)(2,1)} %param.26) | copy-start | bytes 196612
  8.9 6.7 %copy-start.11 = (f32[2048]{0:T(1024)S(1)}, f32[2048]{0:T(1024)}, u32[]{:S(2)}) copy-start(f32[2048]{0:T(1024)} %param.23) | copy-start | bytes 24580
  9.0 7.1 %copy-start.10 = (bf16[16,256]{1,0:T(8,128)(2,1)S(1)}, bf16[16,256]{1,0:T(8,128)(2,1)}, u32[]{:S(2)}) copy-start(bf16[16,256]{1,0:T(8,128)(2,1)} %param.27) | copy-start | bytes 24580
  9.0 7.1 %copy-start.13 = (f32[256]{0:T(256)S(1)}, f32[256]{0:T(256)}, u32[]{:S(2)}) copy-start(f32[256]{0:T(256)} %param.28) | copy-start | bytes 3076
  12.9 0.8 copy-start.4
  13.7 4.1 %collective-permute-start = (bf16[3,1024]{1,0:T(4,128)(2,1)S(1)}, bf16[3,1024]{1,0:T(4,128)(2,1)S(1)}, u32[]{:S(2)}, u32[]{:S(2)}) collective-permute-start(bf16[3,1024]{1,0:T(4,128)(2,1)S(1)} %slice.111), channel_id=1, source_target_pairs={{0,4},{4,8},{8,12},{12,16},{16,20},{20,24},{24,28},{28,32},{32,36}... | collective-permute-start | bytes 18440 | tf_op jit(solution)/shard_map/ppermute | solution.py:40
  44.3 178.8 %reduce-scatter.2.cloned.1.call-start = ((), (), s32[]{:S(2)}) async-start(), calls=%async_computation.2 | async-start | bytes 1310720 | tf_op jit(solution)/shard_map/reduce_scatter | solution.py:257
  139.3 55.9 %copy-start.12 = (f32[512]{0:T(512)S(1)}, f32[512]{0:T(512)}, u32[]{:S(2)}) copy-start(f32[512]{0:T(512)} %param.30) | copy-start | bytes 6148
  198.0 1.8 copy-start.2
  199.8 156.3 %all-reduce.3.cloned.1.call-start = ((), (), s32[]{:S(2)}) async-start(), calls=%async_computation.3 | async-start | bytes 4194304 | tf_op jit(solution)/shard_map/psum | solution.py:278
  224.3 128.4 %copy-start.5 = (bf16[256,512]{1,0:T(8,128)(2,1)}, bf16[256,512]{1,0:T(8,128)(2,1)S(1)}, u32[]{:S(2)}) copy-start(bf16[256,512]{1,0:T(8,128)(2,1)S(1)} %add_convert_fusion) | copy-start | bytes 786436
  352.7 8.9 %all-to-all-start = ((f32[4,8,512]{2,1,0:T(8,128)}), f32[4,8,512]{2,1,0:T(8,128)S(1)}, u32[]{:S(2)}, u32[]{:S(2)}) async-start(f32[4,8,512]{2,1,0:T(8,128)} %stack.6), calls=%async_computation.1 | async-start | bytes 131072 | tf_op jit(solution)/shard_map/all_to_all | solution.py:281
  356.0 6.2 %copy-start.3 = (bf16[250,2048]{1,0:T(8,128)(2,1)S(1)}, bf16[250,2048]{1,0:T(8,128)(2,1)}, u32[]{:S(2)}) copy-start(bf16[250,2048]{1,0:T(8,128)(2,1)} %param.33) | copy-start | bytes 3072004
  356.0 6.2 %copy-start.7 = (f32[2048]{0:T(1024)S(1)}, f32[2048]{0:T(1024)}, u32[]{:S(2)}) copy-start(f32[2048]{0:T(1024)} %param.32) | copy-start | bytes 24580
Sparse Core Ops, SparseCore 0:
  44.4 57.1 all-gather.4
  199.9 23.1 reduce-scatter.1
  227.0 107.2 all-reduce.2
